TPU v7x, 32 devices: a whole 2x2x4 slice. The times are simulated.
32 devices in a mesh: dp: 2 (over y), expert: 16 (over z, x, core).
Axes of the slice: x: 2, y: 2, z: 4, core: 2. Of those that a mesh axis runs over, the one named last changes fastest.
Arguments:
- tokens: bfloat16 [4096, 1024], P(('dp', 'expert')), may hold values from -6 to 6
- masked: int32 [4096], P(('dp', 'expert')), may hold values 0 or 1
- importance: float32 [4096], P(('dp', 'expert')), may hold values from 1 to 10
- routes: int32 [4096, 8], P(('dp', 'expert')), may hold values from 0 to 15, all different within a row; in each aligned block of 128 rows (0 to 127, 128 to 255, ...) at most 96 rows name the same one
- gates: float32 [4096, 8], P(('dp', 'expert')), may hold values from 0.05 to 0.3
- cotangent: bfloat16 [4096, 1024], P(('dp', 'expert')), may hold values from -6 to 6
- w_gate: bfloat16 [16, 512, 1024], P('expert'), may hold values from -0.1875 to 0.1875
- w_up: bfloat16 [16, 512, 1024], P('expert'), may hold values from -0.1875 to 0.1875
- w_down: bfloat16 [16, 512, 1024], P('expert'), may hold values from -0.25 to 0.25
Outputs:
- mixed: bfloat16 [4096, 1024], P(('dp', 'expert'))
- weight_grads: float32 [16, 512, 3, 1024], P('expert', 'dp')
Inputs may be any that keep to these rules, and one draw needn't show every extreme that they name: `routes`: among the 128 rows of one device (aligned blocks of rows), no expert is named by more than 96 rows, a bound that some block reaches; a row names 8 different experts.
All inputs are finite; a program needn't handle non-finite values. No bound on the sum of `masked` on one device may be relied on, other than what follows from the above.
Results may differ from a plain program's by a relative error of at most 0.0057.
Values may be sent and summed in bfloat16 or wider, within the bound.
No kernel may reach another device: no remote copies, remote signals or barrier semaphores. Data moves between devices by JAX's collectives and lax.ppermute only.
A program may use at most 64 MiB of HBM per device.

v0:
```python
import jax
import jax.numpy as jnp
from jax import lax
from jax.sharding import PartitionSpec as P

GATHER_ROWS = 2048
RETURN = "scatter"


def contract_rows(left, right):
    return lax.dot_general(
        left, right, (((0,), (0,)), ((), ())), preferred_element_type=jnp.float32
    )


def contract_cols(left, right):
    return lax.dot_general(
        left, right, (((1,), (1,)), ((), ())), preferred_element_type=jnp.float32
    )


def expert_math(rows_x, rows_q, wgate, wup, wdown):
    gate_pre = contract_cols(rows_x, wgate)
    up_pre = contract_cols(rows_x, wup)
    sig = jax.nn.sigmoid(gate_pre)
    act = gate_pre * sig
    hidden = (act * up_pre).astype(jnp.bfloat16)
    expert_out = jnp.dot(hidden, wdown, preferred_element_type=jnp.float32).astype(jnp.bfloat16)
    back = contract_cols(rows_q, wdown)
    d_gate = (back * up_pre * sig * (1.0 + gate_pre * (1.0 - sig))).astype(jnp.bfloat16)
    d_up = (back * act).astype(jnp.bfloat16)
    grad_gate = contract_rows(d_gate, rows_x)
    grad_up = contract_rows(d_up, rows_x)
    grad_down = contract_rows(hidden, rows_q)
    return (expert_out, jnp.stack([grad_gate, grad_up, grad_down], axis=1))


def reduce_grads(grads, width):
    share = grads.shape[0] // lax.axis_size("dp")
    summed = lax.psum_scatter(grads, "dp", scatter_dimension=0, tiled=True)
    return summed.reshape(1, share, 3, width)


def source_slots(routes, experts):
    flat = routes.reshape(-1)
    onehot = (flat[:, None] == jnp.arange(experts, dtype=jnp.int32)[None, :]).astype(jnp.int32)
    before = jnp.cumsum(onehot, axis=0) - onehot
    return (flat, jnp.sum(before * onehot, axis=1))


def local_a2a(tokens, masked, importance, routes, gates, cotangent, w_gate, w_up, w_down):
    tok_rows = tokens.shape[0]
    width = tokens.shape[1]
    topk = routes.shape[1]
    experts = lax.axis_size("expert")
    capacity = min(tok_rows, 3 * tok_rows * topk // (2 * experts))
    flat, slots = source_slots(routes, experts)
    target = flat * capacity + slots
    owner = jnp.arange(tok_rows * topk, dtype=jnp.int32) // topk
    coef = importance * masked.astype(jnp.float32)
    factor = (coef[:, None] * gates).reshape(-1)
    sent_x = jnp.zeros((experts * capacity, width), jnp.bfloat16).at[target].set(tokens[owner])
    scaled = (factor[:, None] * cotangent[owner].astype(jnp.float32)).astype(jnp.bfloat16)
    sent_q = jnp.zeros((experts * capacity, width), jnp.bfloat16).at[target].set(scaled)
    layout = (experts, capacity, width)
    recv_x = lax.all_to_all(sent_x.reshape(layout), "expert", 0, 0, tiled=True)
    recv_q = lax.all_to_all(sent_q.reshape(layout), "expert", 0, 0, tiled=True)
    expert_out, grads = expert_math(
        recv_x.reshape(-1, width), recv_q.reshape(-1, width), w_gate[0], w_up[0], w_down[0]
    )
    returned = lax.all_to_all(expert_out.reshape(layout), "expert", 0, 0, tiled=True)
    picked = returned.reshape(-1, width)[target].astype(jnp.float32)
    summed = jnp.sum(picked.reshape(tok_rows, topk, width) * gates[:, :, None], axis=1)
    return (summed.astype(jnp.bfloat16), reduce_grads(grads, width))


def local_gather(tokens, masked, importance, routes, gates, cotangent, w_gate, w_up, w_down):
    tok_rows = tokens.shape[0]
    width = tokens.shape[1]
    topk = routes.shape[1]
    experts = lax.axis_size("expert")
    capacity = min(tok_rows, 3 * tok_rows * topk // (2 * experts))
    me = lax.axis_index("expert")
    coef = importance * masked.astype(jnp.float32)
    factor = coef[:, None] * gates
    meta = jnp.concatenate([routes.astype(jnp.float32), factor, gates], axis=1)
    all_x = lax.all_gather(tokens, "expert", axis=0, tiled=True)
    all_meta = lax.all_gather(meta, "expert", axis=0, tiled=True)
    all_c = lax.all_gather(cotangent, "expert", axis=0, tiled=True)
    all_routes = all_meta[:, :topk].astype(jnp.int32)
    hit = all_routes == me
    zero = jnp.zeros((), jnp.float32)
    fac = jnp.sum(jnp.where(hit, all_meta[:, topk : 2 * topk], zero), axis=1)
    gte = jnp.sum(jnp.where(hit, all_meta[:, 2 * topk :], zero), axis=1)
    routed = jnp.any(hit, axis=1).reshape(experts, tok_rows)
    ahead = (
        lax.broadcasted_iota(jnp.int32, (tok_rows, tok_rows), 0)
        < lax.broadcasted_iota(jnp.int32, (tok_rows, tok_rows), 1)
    ).astype(jnp.bfloat16)
    rank = jnp.dot(routed.astype(jnp.bfloat16), ahead, preferred_element_type=jnp.float32).astype(
        jnp.int32
    )
    slot_ids = lax.broadcasted_iota(jnp.int32, (experts, capacity, tok_rows), 1)
    pick = (routed[:, None, :] & (rank[:, None, :] == slot_ids)).astype(jnp.bfloat16)

    def select(values):
        rows = jnp.einsum(
            "sjt,std->sjd",
            pick,
            values.reshape(experts, tok_rows, width),
            preferred_element_type=jnp.float32,
        )
        return rows.astype(jnp.bfloat16).reshape(experts * capacity, width)

    rows_x = select(all_x)
    all_q = (fac[:, None] * all_c.astype(jnp.float32)).astype(jnp.bfloat16)
    rows_q = select(all_q)
    expert_out, grads = expert_math(rows_x, rows_q, w_gate[0], w_up[0], w_down[0])
    if RETURN == "scatter":
        dense = jnp.einsum(
            "sjt,sjd->std",
            pick,
            expert_out.reshape(experts, capacity, width),
            preferred_element_type=jnp.float32,
        ).reshape(experts * tok_rows, width)
        contrib = gte[:, None] * dense
        summed = lax.psum_scatter(contrib, "expert", scatter_dimension=0, tiled=True)
    else:
        returned = lax.all_to_all(
            expert_out.reshape(experts, capacity, width), "expert", 0, 0, tiled=True
        )
        flat, slots = source_slots(routes, experts)
        target = flat * capacity + slots
        choose = (
            target[:, None]
            == lax.broadcasted_iota(jnp.int32, (tok_rows * topk, experts * capacity), 1)
        ).astype(jnp.bfloat16)
        picked = jnp.dot(choose, returned.reshape(-1, width), preferred_element_type=jnp.float32)
        summed = jnp.sum(picked.reshape(tok_rows, topk, width) * gates[:, :, None], axis=1)
    return (summed.astype(jnp.bfloat16), reduce_grads(grads, width))


def local(*args):
    tokens = args[0]
    if lax.axis_size("expert") * tokens.shape[0] <= GATHER_ROWS:
        return local_gather(*args)
    return local_a2a(*args)


def solution(mesh):
    in_specs = (
        P(("dp", "expert"), None),
        P(("dp", "expert")),
        P(("dp", "expert")),
        P(("dp", "expert"), None),
        P(("dp", "expert"), None),
        P(("dp", "expert"), None),
        P("expert", None, None),
        P("expert", None, None),
        P("expert", None, None),
    )
    out_specs = (P(("dp", "expert"), None), P("expert", "dp", None, None))
    return jax.shard_map(local, mesh=mesh, in_specs=in_specs, out_specs=out_specs, check_vma=False)
```

profile of v0, /device:TPU:0, one launch (start us, length us, event | category | flops | bytes accessed | tf_op | source)
XLA Modules:
  0.0 308.5 jit_solution(12384886933002429471)
XLA Ops:
  7.2 0.0 copy-start
  7.2 0.0 all-gather.3.cloned.1.call-start
  7.2 0.7 all-gather.3.cloned.1.call-update
  7.9 0.0 all-gather.5.cloned.1.call-start
  8.0 0.7 all-gather.5.cloned.1.call-update
  8.7 0.0 reduce-scatter.3.cloned.1.call-start
  8.7 0.7 convert_element_type.42
  9.4 0.7 convert_multiply_fusion
  10.1 0.7 broadcast_multiply_fusion
  10.8 0.7 pad_maximum_fusion.1
  11.5 23.8 %all_gather.9 = f32[2048,24]{0,1:T(8,128)S(1)} all-gather(f32[128,24]{0,1:T(8,128)S(1)} %pad_maximum_fusion.1), channel_id=1, replica_groups=mesh['dp'=2,'expert'=16] {'expert'}, dimensions={0}, use_global_device_ids=true | all-gather | bytes 208896 | tf_op jit(solution)/shard_map/all_gather | solution.py:88
  35.3 0.1 fusion.20
  35.4 0.1 convolution_convert_fusion.3
  35.5 28.4 %all-gather.3.cloned.1.call-done = bf16[2048,1024]{1,0:T(8,128)(2,1)} async-done(((bf16[128,1024]{1,0:T(8,128)(2,1)}), bf16[2048,1024]{1,0:T(8,128)(2,1)}) %all-gather.3.cloned.1.call-update) | async-done | bytes 4194320 | tf_op jit(solution)/shard_map/all_gather | solution.py:87
  63.9 0.0 copy-start.3
  63.9 3.2 %convolution_convert_fusion.2 = bf16[16,96,1024]{2,1,0:T(8,128)(2,1)S(1)} fusion(bf16[16,128,1024]{2,1,0:T(8,128)(2,1)} %bitcast.42, s32[16,128]{1,0:T(8,128)S(1)} %convolution_convert_fusion.3, pred[16,128]{1,0:T(8,128)(4,1)S(1)} %bitcast.50), kind=kOutput, calls=%fused_computation.10 | convolution fusion | flops 404619264 | bytes 7350272 | tf_op jit(solution)/shard_map/sjt,std->sjd/dot_general | solution.py:107
  67.2 0.0 copy-start.1
  67.2 0.0 copy-done.3
  67.2 0.0 copy-start.4
  67.2 1.8 fusion.6
  69.0 0.0 copy-done.1
  69.0 0.2 copy-done.4
  69.2 0.0 copy-start.5
  69.2 3.9 %multiply_convert_fusion.3 = (bf16[1536,512]{1,0:T(8,128)(2,1)S(1)}, f32[1536,512]{1,0:T(8,128)}) fusion(f32[1536,512]{1,0:T(8,128)S(1)} %fusion.6, bf16[1536,1024]{1,0:T(8,128)(2,1)S(1)} %bitcast.44, bf16[1,512,1024]{2,1,0:T(8,128)(2,1)S(1)} %copy-done.4), kind=kOutput, calls=%fused_computation.6 | convolution fusion | flops 1615331328 | bytes 12058624 | tf_op jit(solution)/shard_map/dot_general | solution.py:17
  73.2 0.0 copy-done.5
  73.2 0.0 copy-done
  73.2 1.8 convolution_convert_fusion
  75.0 1.3 fusion.10
  76.3 3.9 %bitcast_multiply_fusion = f32[2048,1024]{1,0:T(8,128)} fusion(f32[16,128,1024]{2,1,0:T(8,128)S(1)} %fusion.10, f32[2048]{0:T(1024)S(1)} %get-tuple-element.3), kind=kLoop, calls=%fused_computation | loop fusion | flops 2097152 | bytes 16785408 | tf_op jit(solution)/shard_map/mul | solution.py:126
  80.2 0.0 reduce-scatter.3.cloned.1.call-update
  80.2 0.2 reduce-scatter.5.cloned.1.call-start
  80.4 34.7 %all-gather.5.cloned.1.call-done = bf16[2048,1024]{1,0:T(8,128)(2,1)} async-done(((bf16[128,1024]{1,0:T(8,128)(2,1)}), bf16[2048,1024]{1,0:T(8,128)(2,1)}) %all-gather.5.cloned.1.call-update) | async-done | bytes 4194320 | tf_op jit(solution)/shard_map/all_gather | solution.py:89
  115.1 2.9 multiply_convert_fusion
  118.1 1.0 convolution_convert_fusion.1
  119.1 1.8 fusion.1
  120.9 0.0 copy-start.2
  120.9 0.0 copy-start.6
  120.9 1.8 convolution_bitcast_fusion
  122.8 0.0 copy-done.2
  122.8 1.3 copy-done.6
  124.1 0.0 copy-start.7
  124.1 1.9 convolution_bitcast_fusion.1
  126.0 0.3 copy-done.7
  126.4 2.5 convolution_bitcast_fusion.2
  128.9 3.4 %pad_maximum_fusion = f32[512,3,1024]{2,0,1:T(8,128)} fusion(f32[512,1,1024]{2,0,1:T(8,128)S(1)} %convolution_bitcast_fusion, f32[512,1,1024]{2,0,1:T(8,128)S(1)} %convolution_bitcast_fusion.1, f32[512,1,1024]{2,0,1:T(8,128)S(1)} %convolution_bitcast_fusion.2), kind=kLoop, calls=%fused_computation.2 | loop fusion | flops 3145728 | bytes 12582912 | tf_op jit(solution)/shard_map/stack | solution.py:35
  132.2 0.0 reduce-scatter.5.cloned.1.call-update
  132.2 90.1 %reduce-scatter.3.cloned.1.call-done = f32[128,1024]{1,0:T(8,128)} async-done(((f32[2048,1024]{1,0:T(8,128)}), f32[128,1024]{1,0:T(8,128)}) %reduce-scatter.3.cloned.1.call-update) | async-done | bytes 524304 | tf_op jit(solution)/shard_map/reduce_scatter | solution.py:127
  222.4 1.8 convert_element_type.49
  224.2 77.8 %reduce-scatter.5.cloned.1.call-done = f32[256,3,1024]{2,0,1:T(8,128)} async-done(((f32[512,3,1024]{2,0,1:T(8,128)}), f32[256,3,1024]{2,0,1:T(8,128)}) %reduce-scatter.5.cloned.1.call-update) | async-done | bytes 3145744 | tf_op jit(solution)/shard_map/reduce_scatter | solution.py:40
  (1 shorter events, 0.0 us)
Async XLA Ops:
  7.2 66.0 %copy-start = (bf16[1,512,1024]{2,1,0:T(8,128)(2,1)S(1)}, bf16[1,512,1024]{2,1,0:T(8,128)(2,1)}, u32[]{:S(2)}) copy-start(bf16[1,512,1024]{2,1,0:T(8,128)(2,1)} %param.17) | copy-start | bytes 3145732
  7.2 56.7 %all-gather.3.cloned.1.call-start = ((), (), s32[]{:S(2)}) async-start(), calls=%async_computation.2 | async-start | bytes 4456448 | tf_op jit(solution)/shard_map/all_gather | solution.py:87
  7.9 107.2 %all-gather.5.cloned.1.call-start = ((), (), s32[]{:S(2)}) async-start(), calls=%async_computation.4 | async-start | bytes 4456448 | tf_op jit(solution)/shard_map/all_gather | solution.py:89
  8.7 213.7 %reduce-scatter.3.cloned.1.call-start = ((), (), s32[]{:S(2)}) async-start(), calls=%async_computation.3 | async-start | bytes 8912896 | tf_op jit(solution)/shard_map/reduce_scatter | solution.py:127
  63.9 3.3 %copy-start.3 = (bf16[1,512,1024]{2,1,0:T(8,128)(2,1)S(1)}, bf16[1,512,1024]{2,1,0:T(8,128)(2,1)}, u32[]{:S(2)}) copy-start(bf16[1,512,1024]{2,1,0:T(8,128)(2,1)} %param.15) | copy-start | bytes 3145732
  67.2 1.9 copy-start.1
  67.2 2.0 copy-start.4
  69.2 3.9 %copy-start.5 = (f32[1536,512]{1,0:T(8,128)}, f32[1536,512]{1,0:T(8,128)S(1)}, u32[]{:S(2)}) copy-start(f32[1536,512]{1,0:T(8,128)S(1)} %fusion.6) | copy-start | bytes 9437188
  80.2 221.8 %reduce-scatter.5.cloned.1.call-start = ((), (), s32[]{:S(2)}) async-start(), calls=%async_computation.5 | async-start | bytes 9437184 | tf_op jit(solution)/shard_map/reduce_scatter | solution.py:40
  120.9 1.9 copy-start.2
  120.9 3.2 %copy-start.6 = (f32[1536,512]{1,0:T(8,128)S(1)}, f32[1536,512]{1,0:T(8,128)}, u32[]{:S(2)}) copy-start(f32[1536,512]{1,0:T(8,128)} %copy-done.5) | copy-start | bytes 9437188
  124.1 2.3 copy-start.7
Sparse Core Ops, SparseCore 0:
  10.2 53.6 all-gather.2
  66.1 49.0 all-gather.4
  119.2 103.1 reduce-scatter.2
  225.1 76.7 reduce-scatter.4
where the time goes:
time: 309 us; the launch traced here: 308 us
  waiting for transfers between devices  232 us (75%)
  blocking collectives  23.8 us (8%)
  matrix products  21.4 us (7%)
  other arithmetic  14.7 us (5%)
  between operations  13.9 us (4%)
    reduce_scatter x1, waiting for transfers between devices, local_gather(): lax.psum_scatter(contrib, 'expert', scatter_dimension=0, tiled=True)  90.1 us
    reduce_scatter x1, waiting for transfers between devices, reduce_grads(): summed = lax.psum_scatter(grads, 'dp', scatter_dimension=0, tiled=True)  77.8 us
    all_gather x1, waiting for transfers between devices, local_gather(): all_c = lax.all_gather(cotangent, 'expert', axis=0, tiled=True)  34.7 us
    all_gather x1, waiting for transfers between devices, local_gather(): all_x = lax.all_gather(tokens, 'expert', axis=0, tiled=True)  28.4 us
    all_gather x1, blocking collectives, local_gather(): all_meta = lax.all_gather(meta, 'expert', axis=0, tiled=True)  23.8 us
    dot_general x3, matrix products, contract_cols(): lax.dot_general(left, right, (((1,), (1,)), ((), ())), preferred_element_...  7.63 us
    dot_general x3, matrix products, contract_rows(): lax.dot_general(left, right, (((0,), (0,)), ((), ())), preferred_element_...  6.24 us
  transfers between devices with their start and end apart: 4, of which 4 were waited for; matrix products, arithmetic and copies ran while one was open for 12% of the time, Pallas kernels for 0%

commit v1 on v0

--- a/solution.py
+++ b/solution.py
@@ -85,8 +85,11 @@
     factor = coef[:, None] * gates
     meta = jnp.concatenate([routes.astype(jnp.float32), factor, gates], axis=1)
     all_x = lax.all_gather(tokens, "expert", axis=0, tiled=True)
-    all_meta = lax.all_gather(meta, "expert", axis=0, tiled=True)
-    all_c = lax.all_gather(cotangent, "expert", axis=0, tiled=True)
+    all_meta, all_c = jnp.split(
+        lax.all_gather(jnp.concatenate([meta, cotangent], axis=1), "expert", axis=0, tiled=True),
+        [meta.shape[1]],
+        axis=1,
+    )
     all_routes = all_meta[:, :topk].astype(jnp.int32)
     hit = all_routes == me
     zero = jnp.zeros((), jnp.float32)

time: 309 us -> 356 us (1.15)
  waiting for transfers between devices: 232 us -> 295 us
  blocking collectives: 23.8 us -> 0 us
  local copies, waits for them, and re-layouts: 1.87 us -> 6.05 us
    all_gather x1, waiting for transfers between devices: 34.7 us -> 83.5 us  [local_gather(): lax.all_gather(jnp.concatenate([meta, cotangent], axis=1), 'expert', axis...]
    all_gather x1 -> x0, blocking collectives: 23.8 us -> none  [local_gather(): all_meta = lax.all_gather(meta, 'expert', axis=0, tiled=True)]
    all_gather x1, waiting for transfers between devices: 28.4 us -> 46.9 us  [local_gather(): all_x = lax.all_gather(tokens, 'expert', axis=0, tiled=True)]
    mul x1 -> x0, other arithmetic: 3.85 us -> none  [local_gather(): contrib = gte[:, None] * dense]
    reduce_scatter x1, waiting for transfers between devices: 90.1 us -> 86.3 us  [local_gather(): lax.psum_scatter(contrib, 'expert', scatter_dimension=0, tiled=True)]
  transfers between devices with their start and end apart: 4 -> 4, of which waited for: 4 -> 4; matrix products, arithmetic and copies ran while one was open for 12% -> 6% of each run, Pallas kernels for 0% -> 0%
where the time goes in v1:
time: 356 us
  waiting for transfers between devices  295 us (83%)
  matrix products  23.5 us (7%)
  other arithmetic  16.7 us (5%)
  between operations  13.9 us (4%)
  local copies, waits for them, and re-layouts  6.05 us (2%)
    reduce_scatter x1, waiting for transfers between devices, local_gather(): lax.psum_scatter(contrib, 'expert', scatter_dimension=0, tiled=True)  86.3 us
    all_gather x1, waiting for transfers between devices, local_gather(): lax.all_gather(jnp.concatenate([meta, cotangent], axis=1), 'expert', axis...  83.5 us
    reduce_scatter x1, waiting for transfers between devices, reduce_grads(): summed = lax.psum_scatter(grads, 'dp', scatter_dimension=0, tiled=True)  77.8 us
    all_gather x1, waiting for transfers between devices, local_gather(): all_x = lax.all_gather(tokens, 'expert', axis=0, tiled=True)  46.9 us
    dot_general x3, matrix products, contract_cols(): lax.dot_general(left, right, (((1,), (1,)), ((), ())), preferred_element_...  7.63 us
  transfers between devices with their start and end apart: 4, of which 4 were waited for; matrix products, arithmetic and copies ran while one was open for 6% of the time, Pallas kernels for 0%

profile of v1, /device:TPU:0, one launch (start us, length us, event | category | flops | bytes accessed | tf_op | source)
XLA Modules:
  0.0 355.8 jit_solution(6452393381387110321)
XLA Ops:
  7.2 0.0 copy-start
  7.2 0.0 all-gather.3.cloned.1.call-start
  7.2 0.9 copy.17
  8.1 0.7 convert_multiply_fusion
  8.8 0.7 broadcast_multiply_fusion
  9.5 0.7 convert_element_type.42
  10.1 0.1 copy.15
  10.3 0.1 copy.16
  10.4 2.0 concatenate.3
  12.4 0.0 all-gather.3.cloned.1.call-update
  12.4 0.0 all-gather.5.cloned.1.call-start
  12.5 0.7 all-gather.5.cloned.1.call-update
  13.2 0.0 reduce-scatter.3.cloned.1.call-start
  13.2 83.5 %all-gather.3.cloned.1.call-done = f32[2048,1048]{1,0:T(8,128)} async-done(((f32[128,1048]{1,0:T(8,128)}), f32[2048,1048]{1,0:T(8,128)}) %all-gather.3.cloned.1.call-update) | async-done | bytes 8585232 | tf_op jit(solution)/shard_map/all_gather | solution.py:89
  96.7 3.5 fusion.2
  100.2 0.3 reduce_or.9
  100.6 0.1 convolution_convert_fusion.3
  100.7 46.9 %all-gather.5.cloned.1.call-done = bf16[2048,1024]{1,0:T(8,128)(2,1)} async-done(((bf16[128,1024]{1,0:T(8,128)(2,1)}), bf16[2048,1024]{1,0:T(8,128)(2,1)}) %all-gather.5.cloned.1.call-update) | async-done | bytes 4194320 | tf_op jit(solution)/shard_map/all_gather | solution.py:87
  147.6 0.0 copy-start.3
  147.6 3.2 convolution_convert_fusion.2
  150.9 0.0 copy-start.1
  150.9 0.0 copy-done.3
  150.9 0.0 copy-start.4
  150.9 1.8 fusion.10
  152.7 0.0 copy-done.1
  152.8 0.2 copy-done.4
  152.9 0.0 copy-start.5
  152.9 3.9 %multiply_convert_fusion.2 = (bf16[1536,512]{1,0:T(8,128)(2,1)S(1)}, f32[1536,512]{1,0:T(8,128)}) fusion(f32[1536,512]{1,0:T(8,128)S(1)} %fusion.10, bf16[1536,1024]{1,0:T(8,128)(2,1)S(1)} %bitcast.46, bf16[1,512,1024]{2,1,0:T(8,128)(2,1)S(1)} %copy-done.4), kind=kOutput, calls=%fused_computation.7 | convolution fusion | flops 1615331328 | bytes 12058624 | tf_op jit(solution)/shard_map/dot_general | solution.py:17
  156.9 0.0 copy-done.5
  156.9 0.0 copy-done
  156.9 0.0 slice-start
  156.9 0.0 slice-start.1
  156.9 1.8 convolution_convert_fusion
  158.7 0.0 slice-start.2
  158.7 1.3 fusion.14
  160.0 0.0 slice-done
  160.1 0.3 slice-done.1
  160.3 0.4 slice-done.2
  160.8 5.6 %fusion = (bf16[2048,1024]{1,0:T(8,128)(2,1)}, f32[2048,1024]{1,0:T(8,128)}) fusion(f32[2048,1048]{1,0:T(8,128)S(1)} %bitcast.43, f32[2048]{0:T(1024)S(1)} %get-tuple-element.2, f32[16,128,1024]{2,1,0:T(8,128)S(1)} %fusion.14, f32[2048]{0:T(1024)S(1)} %get-tuple-element.3), kind=kLoop, calls=%fused_computation.1 | loop fusion | flops 6291456 | bytes 29376512 | tf_op jit(solution)/shard_map/convert_element_type | solution.py:119
  166.4 0.0 reduce-scatter.3.cloned.1.call-update
  166.4 0.2 reduce-scatter.5.cloned.1.call-start
  166.6 3.2 convolution_convert_fusion.1
  169.8 1.8 fusion.5
  171.7 0.0 copy-start.2
  171.7 0.0 copy-start.6
  171.7 1.8 convolution_bitcast_fusion
  173.5 0.4 copy-done.2
  173.9 1.3 copy-done.6
  175.2 0.0 copy-start.7
  175.2 1.9 convolution_bitcast_fusion.1
  177.1 0.3 copy-done.7
  177.5 2.5 convolution_bitcast_fusion.2
  180.0 3.4 pad_maximum_fusion
  183.3 0.0 reduce-scatter.5.cloned.1.call-update
  183.4 86.3 %reduce-scatter.3.cloned.1.call-done = f32[128,1024]{1,0:T(8,128)} async-done(((f32[2048,1024]{1,0:T(8,128)}), f32[128,1024]{1,0:T(8,128)}) %reduce-scatter.3.cloned.1.call-update) | async-done | bytes 524304 | tf_op jit(solution)/shard_map/reduce_scatter | solution.py:130
  269.7 1.8 convert_element_type.50
  271.4 77.8 %reduce-scatter.5.cloned.1.call-done = f32[256,3,1024]{2,0,1:T(8,128)} async-done(((f32[512,3,1024]{2,0,1:T(8,128)}), f32[256,3,1024]{2,0,1:T(8,128)}) %reduce-scatter.5.cloned.1.call-update) | async-done | bytes 3145744 | tf_op jit(solution)/shard_map/reduce_scatter | solution.py:40
  (1 shorter events, 0.0 us)
Async XLA Ops:
  7.2 149.7 %copy-start = (bf16[1,512,1024]{2,1,0:T(8,128)(2,1)S(1)}, bf16[1,512,1024]{2,1,0:T(8,128)(2,1)}, u32[]{:S(2)}) copy-start(bf16[1,512,1024]{2,1,0:T(8,128)(2,1)} %param.17) | copy-start | bytes 3145732
  7.2 89.5 %all-gather.3.cloned.1.call-start = ((), (), s32[]{:S(2)}) async-start(), calls=%async_computation.2 | async-start | bytes 10027008 | tf_op jit(solution)/shard_map/all_gather | solution.py:89
  12.4 135.2 %all-gather.5.cloned.1.call-start = ((), (), s32[]{:S(2)}) async-start(), calls=%async_computation.3 | async-start | bytes 4456448 | tf_op jit(solution)/shard_map/all_gather | solution.py:87
  13.2 256.5 %reduce-scatter.3.cloned.1.call-start = ((), (), s32[]{:S(2)}) async-start(), calls=%async_computation.4 | async-start | bytes 8912896 | tf_op jit(solution)/shard_map/reduce_scatter | solution.py:130
  147.6 3.3 copy-start.3
  150.9 1.9 copy-start.1
  150.9 2.0 copy-start.4
  152.9 3.9 %copy-start.5 = (f32[1536,512]{1,0:T(8,128)}, f32[1536,512]{1,0:T(8,128)S(1)}, u32[]{:S(2)}) copy-start(f32[1536,512]{1,0:T(8,128)S(1)} %fusion.10) | copy-start | bytes 9437188
  156.9 3.2 slice-start
  156.9 3.5 slice-start.1
  158.7 2.0 slice-start.2
  166.4 182.9 %reduce-scatter.5.cloned.1.call-start = ((), (), s32[]{:S(2)}) async-start(), calls=%async_computation.5 | async-start | bytes 9437184 | tf_op jit(solution)/shard_map/reduce_scatter | solution.py:40
  171.7 2.3 copy-start.2
  171.7 3.6 %copy-start.6 = (f32[1536,512]{1,0:T(8,128)S(1)}, f32[1536,512]{1,0:T(8,128)}, u32[]{:S(2)}) copy-start(f32[1536,512]{1,0:T(8,128)} %copy-done.5) | copy-start | bytes 9437188
  175.2 2.2 copy-start.7
Sparse Core Ops, SparseCore 0:
  12.5 84.1 all-gather.2
  98.9 48.7 all-gather.4
  166.5 103.0 reduce-scatter.2
  272.4 76.8 reduce-scatter.4
